TPU v7x, 32 devices: a whole 2x2x4 slice. The times are simulated.
32 devices in a mesh: groups: 2 (over y), blk: 4 (over z), pool: 4 (over x, core).
Axes of the slice: x: 2, y: 2, z: 4, core: 2. Of those that a mesh axis runs over, the one named last changes fastest.
Arguments:
- q_new: bfloat16 [1024, 8192], P(('groups', 'blk'), 'pool'), parts along dimension 0, may hold values from -64 to 64
- kv_new: bfloat16 [1024, 8, 256], P(('groups', 'blk'), 'pool'), parts along dimension 0, may hold values from -7 to 7
- kv_cache: bfloat16 [256, 8, 128, 256], P(('groups', 'blk'), 'pool'), parts along dimension 0, may hold values from -4.5 to 4.5
- page_table: int32 [16], P('groups'), parts along dimension 0, may hold values from 0 to 127, as said below
- block_offsets: int32 [8], P('groups'), parts along dimension 0, may hold values from 0 to 3, each once
Outputs:
- attended: bfloat16 [1024, 8192], P(('groups', 'blk'), 'pool'), parts along dimension 0
There are 2 independent parts, one for each index of `groups`. A program takes and returns all parts, laid end to end along the dimension named above; each array names one. Nothing has to cross between parts.
Inputs may be any that keep to these rules, and one draw needn't show every extreme that they name: `page_table`: distinct slots; slot s lies on blk index s // 32; at most 4 entries lie on the slots of one blk index, and exactly 4 on some blk index.
All inputs are finite; a program needn't handle non-finite values.
Results may differ from a plain program's by a relative error of at most 0.0045.
Values may be sent and summed in bfloat16 or wider, within the bound.
No kernel may reach another device: no remote copies, remote signals or barrier semaphores. Data moves between devices by JAX's collectives and lax.ppermute only.
A program may use at most 64 MiB of HBM per device.

v0:
```python
import math
import jax
import jax.numpy as jnp
from jax import lax
from jax.sharding import PartitionSpec as P

CAP = 4


def attend(running, queries, keys, values, visible, head_size):
    maxima, totals, summed = running
    score_scale = 1.0 / math.sqrt(head_size)
    scores = (
        jnp.einsum("gqd,gkd->gqk", queries, keys, preferred_element_type=jnp.float32) * score_scale
    )
    scores = jnp.where(visible, scores, -1e30)
    row_top = jnp.maximum(maxima, jnp.max(scores, axis=2))
    factor = jnp.exp(maxima - row_top)
    weights = jnp.where(visible, jnp.exp(scores - row_top[..., None]), 0.0)
    totals = totals * factor + jnp.sum(weights, axis=2)
    summed = summed * factor[..., None] + jnp.einsum(
        "gqk,gkd->gqd", weights.astype(jnp.bfloat16), values, preferred_element_type=jnp.float32
    )
    return (row_top, totals, summed)


def local(q_new, kv_new, kv_cache, page_table, block_offsets):
    q_rows = q_new.shape[0]
    kv_heads = kv_new.shape[1]
    head_size = kv_new.shape[2] // 2
    group_size = q_new.shape[1] // (head_size * kv_heads)
    slots_dev = kv_cache.shape[0]
    page_len = kv_cache.shape[2]
    npages = page_table.shape[0]
    blocks = lax.axis_size("blk")
    myself = lax.axis_index("blk")
    pg = -(-npages // blocks)
    block_ids = jnp.arange(blocks, dtype=jnp.int32)
    my_offset = jnp.sum(jnp.where(block_ids == myself, block_offsets, 0))
    query_pos = jnp.tile(my_offset * q_rows + jnp.arange(q_rows, dtype=jnp.int32), group_size)
    queries = (
        q_new.reshape(q_rows, kv_heads, group_size, head_size)
        .transpose(1, 2, 0, 3)
        .reshape(kv_heads, group_size * q_rows, head_size)
    )
    query_span = group_size * q_rows
    page_owner = page_table // slots_dev
    owned = page_owner == myself
    page_rank = jnp.cumsum(owned.astype(jnp.int32)) - 1
    local_slot = page_table % slots_dev
    counts = jnp.sum((page_owner[None, :] == block_ids[:, None]).astype(jnp.int32), axis=1)
    per_peer = (CAP + blocks - 1) // blocks
    starts = jnp.cumsum(counts) - counts
    my_start = jnp.sum(jnp.where(block_ids == myself, starts, 0))
    peer_slots = jnp.arange(per_peer, dtype=jnp.int32)[None, :]
    wanted = (block_ids[:, None] - my_start) % blocks + peer_slots * blocks
    picked = owned[None, None, :] & (page_rank[None, None, :] == wanted[..., None])
    chosen = jnp.sum(jnp.where(picked, local_slot[None, None, :], 0), axis=2).reshape(-1)
    sent_pages = kv_cache[chosen].reshape(blocks, per_peer, kv_heads, page_len, 2 * head_size)
    sent_pages = sent_pages.transpose(0, 2, 1, 3, 4).reshape(
        blocks, kv_heads, per_peer * page_len, 2 * head_size
    )
    own_rows = jnp.broadcast_to(
        kv_new.transpose(1, 0, 2)[None], (blocks, kv_heads, q_rows, 2 * head_size)
    )
    payload = jnp.concatenate([sent_pages, own_rows], axis=2)
    received = lax.all_to_all(payload, "blk", split_axis=0, concat_axis=0, tiled=True)
    page_part = received[:, :, : per_peer * page_len]
    page_part = page_part.reshape(blocks, kv_heads, per_peer, page_len, 2 * head_size)
    page_part = page_part.transpose(0, 2, 1, 3, 4).reshape(
        blocks * per_peer, kv_heads, page_len, 2 * head_size
    )
    arriving = (myself - starts[:, None]) % blocks + peer_slots * blocks
    present = (arriving < counts[:, None]).reshape(-1)
    order_rank = jnp.cumsum(present.astype(jnp.int32)) - 1
    choose = present[None, :] & (order_rank[None, :] == jnp.arange(pg, dtype=jnp.int32)[:, None])
    positions = jnp.sum(
        jnp.where(choose, jnp.arange(blocks * per_peer, dtype=jnp.int32)[None, :], 0), axis=1
    )
    compact = page_part[positions]
    compact_valid = jnp.arange(pg, dtype=jnp.int32) * blocks + myself < npages
    gathered = lax.all_gather(compact, "blk", axis=0, tiled=True)
    gathered_valid = (
        jnp.arange(pg, dtype=jnp.int32)[None, :] * blocks + block_ids[:, None] < npages
    ).reshape(-1)
    new_rows = received[:, :, per_peer * page_len :]
    new_rows = new_rows.transpose(1, 0, 2, 3).reshape(kv_heads, blocks * q_rows, 2 * head_size)
    own_pages = compact.transpose(1, 0, 2, 3).reshape(kv_heads, pg * page_len, 2 * head_size)
    entries_a = jnp.concatenate([new_rows, own_pages], axis=1)
    row_source = jnp.repeat(block_ids, q_rows)
    key_pos = jnp.sum(
        jnp.where(row_source[:, None] == block_ids[None, :], block_offsets[None, :], 0), axis=1
    ) * q_rows + jnp.tile(jnp.arange(q_rows, dtype=jnp.int32), blocks)
    visible_new = key_pos[None, :] <= query_pos[:, None]
    visible_own = jnp.broadcast_to(
        jnp.repeat(compact_valid, page_len)[None, :], (query_span, pg * page_len)
    )
    visible_a = jnp.concatenate([visible_new, visible_own], axis=1)[None]
    running = (
        jnp.full((kv_heads, query_span), -1e30, jnp.float32),
        jnp.zeros((kv_heads, query_span), jnp.float32),
        jnp.zeros((kv_heads, query_span, head_size), jnp.float32),
    )
    running = attend(
        running,
        queries,
        entries_a[..., :head_size],
        entries_a[..., head_size:],
        visible_a,
        head_size,
    )
    page_block = jnp.repeat(block_ids, pg)
    use_page = gathered_valid & (page_block != myself)
    entries_b = gathered.transpose(1, 0, 2, 3).reshape(
        kv_heads, blocks * pg * page_len, 2 * head_size
    )
    visible_b = jnp.repeat(use_page, page_len)[None, None, :]
    running = attend(
        running,
        queries,
        entries_b[..., :head_size],
        entries_b[..., head_size:],
        visible_b,
        head_size,
    )
    maxima, totals, summed = running
    attended = (summed / totals[..., None]).astype(jnp.bfloat16)
    attended = attended.reshape(kv_heads, group_size, q_rows, head_size).transpose(2, 0, 1, 3)
    return attended.reshape(q_rows, kv_heads * group_size * head_size)


def solution(mesh):
    return jax.shard_map(
        local,
        mesh=mesh,
        in_specs=(
            P(("groups", "blk"), "pool"),
            P(("groups", "blk"), "pool", None),
            P(("groups", "blk"), "pool", None, None),
            P("groups"),
            P("groups"),
        ),
        out_specs=P(("groups", "blk"), "pool"),
        check_vma=False,
    )
```

profile of v0, /device:TPU:0, one launch (start us, length us, event | category | flops | bytes accessed | tf_op | source)
XLA Modules:
  0.0 97.5 jit_solution(11759745901006424764)
XLA Ops:
  6.5 0.7 and_select_fusion.3
  7.3 0.7 convert_bitcast_fusion
  8.4 1.4 %fusion.35 = (s32[]{:T(128)}, s32[]{:T(128)}) fusion(s32[4]{0:T(128)} %param.9, s32[]{:T(128)S(6)} %axis_index.15, s32[4]{0:T(128)S(1)} %convert_reduce_fusion, s32[4,1]{0,1:T(1,128)S(1)} %reduce-window.22), kind=kLoop, calls=%fused_computation.78 | loop fusion | flops 22 | bytes 60 | tf_op jit(solution)/shard_map/reduce_sum | solution.py:39
  9.8 0.7 and_select_fusion.4
  10.5 0.2 select_reduce_fusion.1
  10.7 0.9 copy.22
  11.6 2.8 %gather_fusion = bf16[4,2,128,256]{3,2,1,0:T(8,128)(2,1)S(1)} fusion(bf16[32,2,128,256]{3,2,1,0:T(8,128)(2,1)} %param.7, s32[1024]{0:T(1024)S(1)} %pad_clamp_fusion.1), kind=kCustom, calls=%fused_computation | custom fusion | bytes 1048592 | tf_op jit(solution)/shard_map/gather | solution.py:59
  14.4 1.1 %pad_maximum_fusion = bf16[4,2,256,256]{3,2,1,0:T(8,128)(2,1)} fusion(bf16[4,2,128,256]{3,2,1,0:T(8,128)(2,1)S(1)} %broadcast_in_dim.150, bf16[4,2,128,256]{3,2,1,0:T(8,128)(2,1)S(1)} %gather_fusion), kind=kLoop, calls=%fused_computation.23 | loop fusion | flops 2097152 | bytes 2097152 | tf_op jit(solution)/shard_map/concatenate | solution.py:66
  15.5 6.3 %all-to-all-start = ((bf16[4,2,256,256]{3,2,1,0:T(8,128)(2,1)}), bf16[4,2,256,256]{3,2,1,0:T(8,128)(2,1)S(1)}, u32[]{:S(2)}, u32[]{:S(2)}) async-start(bf16[4,2,256,256]{3,2,1,0:T(8,128)(2,1)} %pad_maximum_fusion), calls=%async_computation | async-start | bytes 2097152 | tf_op jit(solution)/shard_map/all_to_all | solution.py:67
  23.4 24.1 %all-to-all-done = bf16[4,2,256,256]{3,2,1,0:T(8,128)(2,1)S(1)} async-done(((bf16[4,2,256,256]{3,2,1,0:T(8,128)(2,1)}), bf16[4,2,256,256]{3,2,1,0:T(8,128)(2,1)S(1)}, u32[]{:S(2)}, u32[]{:S(2)}) %all-to-all-start) | async-done | bytes 1048608 | tf_op jit(solution)/shard_map/all_to_all | solution.py:67
  47.7 1.3 %gather_fusion.1 = bf16[2,2,128,256]{3,2,1,0:T(8,128)(2,1)} fusion(bf16[4,2,128,256]{3,2,1,0:T(8,128)(2,1)S(1)} %get-tuple-element.10, s32[1024]{0:T(1024)S(1)} %pad_clamp_fusion), kind=kCustom, calls=%fused_computation.1 | custom fusion | bytes 524296 | tf_op jit(solution)/shard_map/gather | solution.py:80
  49.0 0.4 broadcast_compare_fusion
  49.4 0.4 pad_add_fusion
  49.8 1.0 copy.24
  50.8 4.0 %fusion.4 = (f32[2,1024]{1,0:T(2,128)S(1)}, f32[2,768,1024]{2,1,0:T(8,128)}) fusion(pred[1024,768]{0,1:T(8,128)(4,1)S(1)} %pad_add_fusion, bf16[2,1024,128]{2,1,0:T(8,128)(2,1)S(1)} %bitcast.92, bf16[2,512,256]{2,1,0:T(8,128)(2,1)S(1)} %bitcast.98, bf16[2,256,256]{2,1,0:T(8,128)(2,1)S(1)} %bitcast.101), kind=kOutput, calls=%fused_computation.11 | convolution fusion | flops 408156160 | bytes 8396800 | tf_op jit(solution)/shard_map/gqd,gkd->gqk/dot_general | solution.py:14
  54.9 21.3 %all-gather.3.cloned.1.call-done = bf16[8,2,128,256]{3,2,1,0:T(8,128)(2,1)} async-done(((bf16[2,2,128,256]{3,2,1,0:T(8,128)(2,1)}), bf16[8,2,128,256]{3,2,1,0:T(8,128)(2,1)}) %all-gather.3.cloned.1.call-update) | async-done | bytes 1048592 | tf_op jit(solution)/shard_map/all_gather | solution.py:82
  76.1 1.3 %copy.27 = bf16[2,8,128,256]{3,2,1,0:T(8,128)(2,1)S(1)} copy(bf16[2,8,128,256]{3,2,0,1:T(8,128)(2,1)} %bitcast.96) | data formatting | bytes 2097152 | tf_op jit(solution)/shard_map/transpose | solution.py:114
  77.5 1.9 %bitcast_reduce_fusion = (f32[2,1024]{1,0:T(2,128)S(1)}, f32[2,1024,1024]{2,1,0:T(8,128)S(1)}) fusion(pred[1024]{0:T(1024)(128)(4,1)S(1)} %broadcast_bitcast_fusion.1, bf16[2,1024,128]{2,1,0:T(8,128)(2,1)S(1)} %bitcast.93, bf16[2,1024,256]{2,1,0:T(8,128)(2,1)S(1)} %bitcast.89), kind=kOutput, calls=%fused_computation.3 | convolution fusion | flops 543160320 | bytes 9446400 | tf_op jit(solution)/shard_map/gqd,gkd->gqk/dot_general | solution.py:14
  79.4 2.5 %fusion.2 = f32[2,1024]{1,0:T(2,128)S(1)} fusion(f32[2,1024,1024]{2,1,0:T(8,128)S(1)} %get-tuple-element.18, f32[2,1024]{1,0:T(2,128)S(1)} %get-tuple-element.13, pred[1024]{0:T(1024)(128)(4,1)S(1)} %broadcast_bitcast_fusion.1), kind=kLoop, calls=%fused_computation.9 | loop fusion | flops 10483712 | bytes 8406016 | tf_op jit(solution)/shard_map/reduce_sum | solution.py:20
  81.9 1.7 %fusion.5 = f32[2,1024]{1,0:T(2,128)S(1)} fusion(f32[2,768,1024]{2,1,0:T(8,128)S(1)} %bitcast.88, f32[2,1024]{1,0:T(2,128)S(1)} %get-tuple-element.14, pred[1024,768]{0,1:T(8,128)(4,1)S(1)} %pad_add_fusion), kind=kLoop, calls=%fused_computation.12 | loop fusion | flops 7862272 | bytes 7094272 | tf_op jit(solution)/shard_map/reduce_sum | solution.py:20
  83.6 2.8 %fusion.20 = f32[2,1024,128]{2,1,0:T(8,128)S(1)} fusion(f32[2,768,1024]{2,1,0:T(8,128)S(1)} %bitcast.88, f32[2,1024]{1,0:T(2,128)S(1)} %get-tuple-element.14, pred[1024,768]{0,1:T(8,128)(4,1)S(1)} %pad_add_fusion, f32[2,1024]{1,0:T(2,128)S(1)} %get-tuple-element.6, f32[2,1024]{1,0:T(2,128)S(1)} %get-tuple-element.12, ...), kind=kOutput, calls=%fused_computation.22 | convolution fusion | flops 411828224 | bytes 8937472 | tf_op jit(solution)/shard_map/gqk,gkd->gqd/dot_general | solution.py:21
  86.4 3.0 %divide_convert_fusion = bf16[2,1024,128]{2,1,0:T(8,128)(2,1)S(1)} fusion(f32[2,1024,128]{2,1,0:T(8,128)S(1)} %fusion.20, f32[2,1024,1024]{2,1,0:T(8,128)S(1)} %get-tuple-element.18, f32[2,1024]{1,0:T(2,128)S(1)} %get-tuple-element.13, pred[1024]{0:T(1024)(128)(4,1)S(1)} %broadcast_bitcast_fusion.1, bf16[2,1024,256]{2,1,0:T(8,128)(2,1)S(1)} %bitcast.90, ...), kind=kOutput, calls=%fused_computation.24 | convolution fusion | flops 548143104 | bytes 10504192 | tf_op jit(solution)/shard_map/gqk,gkd->gqd/dot_general | solution.py:21
  89.4 0.3 copy.29
  89.8 0.9 copy.35
  (43 shorter events, 1.7 us)
Async XLA Ops:
  6.5 16.8 %copy-start.1 = (s32[4]{0:T(128)S(1)}, s32[4]{0:T(128)}, u32[]{:S(2)}) copy-start(s32[4]{0:T(128)} %param.9) | copy-start | bytes 52
  6.5 15.6 %copy-start = (bf16[128,2048]{1,0:T(8,128)(2,1)S(1)}, bf16[128,2048]{1,0:T(8,128)(2,1)}, u32[]{:S(2)}) copy-start(bf16[128,2048]{1,0:T(8,128)(2,1)} %param.5) | copy-start | bytes 1572868
  15.5 32.0 %all-to-all-start = ((bf16[4,2,256,256]{3,2,1,0:T(8,128)(2,1)}), bf16[4,2,256,256]{3,2,1,0:T(8,128)(2,1)S(1)}, u32[]{:S(2)}, u32[]{:S(2)}) async-start(bf16[4,2,256,256]{3,2,1,0:T(8,128)(2,1)} %pad_maximum_fusion), calls=%async_computation | async-start | bytes 2097152 | tf_op jit(solution)/shard_map/all_to_all | solution.py:67
  21.8 54.3 %all-gather.3.cloned.1.call-start = ((), (), s32[]{:S(2)}) async-start(), calls=%async_computation.1 | async-start | bytes 1310720 | tf_op jit(solution)/shard_map/all_gather | solution.py:82
  77.4 4.5 %slice-start = ((s8[6291456]{0:T(1024)(128)(4,1)}), s8[4194304]{0:T(1024)(128)(4,1)S(1)}, s32[]{:S(2)}) async-start(s8[6291456]{0:T(1024)(128)(4,1)} %bitcast.87), calls=%async_computation.2 | async-start | bytes 8388608
  77.4 4.5 %slice-start.1 = ((s8[6291456]{0:T(1024)(128)(4,1)}), s8[2097152]{0:T(1024)(128)(4,1)S(1)}, s32[]{:S(2)}) async-start(s8[6291456]{0:T(1024)(128)(4,1)} %bitcast.87), calls=%async_computation.3 | async-start | bytes 4194304
Sparse Core Ops, SparseCore 0:
  49.1 27.0 all-gather.2
where the time goes:
time: 97.9 us; the launch traced here: 97.5 us
  waiting for transfers between devices  45.4 us (46%)
  between operations  14.3 us (15%)
  matrix products  11.7 us (12%)
  other arithmetic  10.6 us (11%)
  local copies, waits for them, and re-layouts  9.17 us (9%)
  starting transfers between devices  6.32 us (6%)
    all_to_all x1, waiting for transfers between devices, local(): lax.all_to_all(payload, 'blk', split_axis=0, concat_axis=0, tiled=True)  24.1 us
    all_gather x1, waiting for transfers between devices, local(): gathered = lax.all_gather(compact, 'blk', axis=0, tiled=True)  21.3 us
    all_to_all x1, starting transfers between devices, local(): lax.all_to_all(payload, 'blk', split_axis=0, concat_axis=0, tiled=True)  6.32 us
    dot_general x2, matrix products, attend(): jnp.einsum('gqd,gkd->gqk', queries, keys, preferred_element_type=jnp.floa...  5.92 us
    dot_general x2, matrix products, attend(): jnp.einsum('gqk,gkd->gqd', weights.astype(jnp.bfloat16), values, preferre...  5.81 us
    reduce_sum x2, other arithmetic, attend(): totals = totals * factor + jnp.sum(weights, axis=2)  4.16 us
    gather x1, local copies, waits for them, and re-layouts, local(): kv_cache[chosen]  2.77 us
  transfers between devices with their start and end apart: 2, of which 2 were waited for; matrix products, arithmetic and copies ran while one was open for 7% of the time, Pallas kernels for 0%

commit v1 on v0

--- a/solution.py
+++ b/solution.py
@@ -5,6 +5,22 @@
 from jax.sharding import PartitionSpec as P
 
 CAP = 4
+
+
+def exchange_in_pairs(value, axis, split, join):
+    ways, here = (lax.axis_size(axis), lax.axis_index(axis))
+    width = value.shape[split] // ways
+    shape = list(value.shape)
+    shape[split] = width
+    height = shape[join]
+    shape[join] = height * ways
+    full = jnp.zeros(shape, value.dtype)
+    for mask in range(ways):
+        part = lax.dynamic_slice_in_dim(value, (here ^ mask) * width, width, axis=split)
+        if mask:
+            part = lax.ppermute(part, axis, [(d, d ^ mask) for d in range(ways)])
+        full = lax.dynamic_update_slice_in_dim(full, part, (here ^ mask) * height, axis=join)
+    return full
 
 
 def attend(running, queries, keys, values, visible, head_size):
@@ -64,7 +80,7 @@
         kv_new.transpose(1, 0, 2)[None], (blocks, kv_heads, q_rows, 2 * head_size)
     )
     payload = jnp.concatenate([sent_pages, own_rows], axis=2)
-    received = lax.all_to_all(payload, "blk", split_axis=0, concat_axis=0, tiled=True)
+    received = exchange_in_pairs(payload, "blk", 0, 0)
     page_part = received[:, :, : per_peer * page_len]
     page_part = page_part.reshape(blocks, kv_heads, per_peer, page_len, 2 * head_size)
     page_part = page_part.transpose(0, 2, 1, 3, 4).reshape(

time: 97.9 us -> 94 us (0.960)
  waiting for transfers between devices: 45.4 us -> 40.6 us
  local copies, waits for them, and re-layouts: 9.17 us -> 10.3 us
    all_to_all x1 -> x0, waiting for transfers between devices: 24.1 us -> none  [local(): lax.all_to_all(payload, 'blk', split_axis=0, concat_axis=0, tiled=True)]
    ppermute x0 -> x3, waiting for transfers between devices: none -> 18.3 us  [exchange_in_pairs(): part = lax.ppermute(part, axis, [(d, d ^ mask) for d in range(ways)])]
    all_to_all x1 -> x0, starting transfers between devices: 6.32 us -> none  [local(): lax.all_to_all(payload, 'blk', split_axis=0, concat_axis=0, tiled=True)]
    ppermute x0 -> x3, starting transfers between devices: none -> 5.76 us  [exchange_in_pairs(): part = lax.ppermute(part, axis, [(d, d ^ mask) for d in range(ways)])]
    select_n x1, other arithmetic: 0.7 us -> 2.02 us  [local(): wanted = (block_ids[:, None] - my_start) % blocks + peer_slots * blocks]
    unnamed x10 -> x6, local copies, waits for them, and re-layouts: 1.06 us -> 2.09 us
    all_gather x1, waiting for transfers between devices: 21.3 us -> 22.3 us  [local(): gathered = lax.all_gather(compact, 'blk', axis=0, tiled=True)]
  transfers between devices with their start and end apart: 2 -> 4, of which waited for: 2 -> 3; matrix products, arithmetic and copies ran while one was open for 7% -> 9% of each run, Pallas kernels for 0% -> 0%
where the time goes in v1:
time: 94 us; the launch traced here: 93.6 us
  waiting for transfers between devices  40.6 us (43%)
  between operations  14.3 us (15%)
  matrix products  11.7 us (12%)
  other arithmetic  10.8 us (11%)
  local copies, waits for them, and re-layouts  10.3 us (11%)
  starting transfers between devices  5.76 us (6%)
    all_gather x1, waiting for transfers between devices, local(): gathered = lax.all_gather(compact, 'blk', axis=0, tiled=True)  22.3 us
    ppermute x3, waiting for transfers between devices, exchange_in_pairs(): part = lax.ppermute(part, axis, [(d, d ^ mask) for d in range(ways)])  18.3 us
    dot_general x2, matrix products, attend(): jnp.einsum('gqd,gkd->gqk', queries, keys, preferred_element_type=jnp.floa...  5.92 us
    dot_general x2, matrix products, attend(): jnp.einsum('gqk,gkd->gqd', weights.astype(jnp.bfloat16), values, preferre...  5.81 us
    ppermute x3, starting transfers between devices, exchange_in_pairs(): part = lax.ppermute(part, axis, [(d, d ^ mask) for d in range(ways)])  5.76 us
    reduce_sum x2, other arithmetic, attend(): totals = totals * factor + jnp.sum(weights, axis=2)  4.16 us
    gather x1, local copies, waits for them, and re-layouts, local(): kv_cache[chosen]  2.77 us
    unnamed x6, local copies, waits for them, and re-layouts  2.09 us
  transfers between devices with their start and end apart: 4, of which 3 were waited for; matrix products, arithmetic and copies ran while one was open for 9% of the time, Pallas kernels for 0%

profile of v1, /device:TPU:0, one launch (start us, length us, event | category | flops | bytes accessed | tf_op | source)
XLA Modules:
  0.0 93.6 jit_solution(13628126423432896177)
XLA Ops:
  6.5 0.7 and_select_fusion.3
  7.2 0.7 convert_bitcast_fusion
  8.4 0.6 fusion.41
  9.0 2.0 %and_select_fusion.4 = (s32[4]{0:T(128)S(1)}, s32[]{:T(128)}) fusion(s32[]{:T(128)} %fusion.41, s32[4]{0:T(128)} %param.9, s32[]{:T(128)S(6)} %axis_index.19), kind=kLoop, calls=%fused_computation.82 | loop fusion | flops 59 | bytes 44 | tf_op jit(solution)/shard_map/jit(remainder)/select_n | solution.py:72
  11.2 0.9 copy.31
  12.2 2.8 %gather_fusion = bf16[4,2,128,256]{3,2,1,0:T(8,128)(2,1)S(1)} fusion(bf16[32,2,128,256]{3,2,1,0:T(8,128)(2,1)} %param.7, s32[1024]{0:T(1024)S(1)} %pad_clamp_fusion.1), kind=kCustom, calls=%fused_computation | custom fusion | bytes 1048592 | tf_op jit(solution)/shard_map/gather | solution.py:75
  15.1 5.1 %collective-permute-start.2 = (bf16[1,2,256,256]{3,2,1,0:T(8,128)(2,1)S(1)}, bf16[1,2,256,256]{3,2,1,0:T(8,128)(2,1)S(1)}, u32[]{:S(2)}, u32[]{:S(2)}) collective-permute-start(bf16[1,2,256,256]{3,2,1,0:T(8,128)(2,1)S(1)} %get-tuple-element.12), channel_id=1, source_target_pairs={{0,12},{4,8},{8,4},{12,0},{1,13},{5,9},{9,5},{13,1},{2,14},{6,10},... | collective-permute-start | bytes 786440 | tf_op jit(solution)/shard_map/ppermute | solution.py:21
  20.3 0.6 collective-permute-start.1
  21.4 0.7 select_reduce_fusion
  22.9 1.1 %copy.41 = bf16[16,8,16,128]{3,2,1,0:T(8,128)(2,1)S(1)} copy(bf16[16,8,16,128]{3,1,2,0:T(8,128)(2,1)} %bitcast.97) | data formatting | bytes 1048576
  24.2 9.1 %collective-permute-done = bf16[1,2,256,256]{3,2,1,0:T(8,128)(2,1)S(1)} collective-permute-done((bf16[1,2,256,256]{3,2,1,0:T(8,128)(2,1)S(1)}, bf16[1,2,256,256]{3,2,1,0:T(8,128)(2,1)S(1)}, u32[]{:S(2)}, u32[]{:S(2)}) %collective-permute-start) | collective-permute-done | bytes 262176 | tf_op jit(solution)/shard_map/ppermute | solution.py:21
  33.3 9.2 %collective-permute-done.1 = bf16[1,2,256,256]{3,2,1,0:T(8,128)(2,1)S(1)} collective-permute-done((bf16[1,2,256,256]{3,2,1,0:T(8,128)(2,1)S(1)}, bf16[1,2,256,256]{3,2,1,0:T(8,128)(2,1)S(1)}, u32[]{:S(2)}, u32[]{:S(2)}) %collective-permute-start.1) | collective-permute-done | bytes 262176 | tf_op jit(solution)/shard_map/ppermute | solution.py:21
  42.7 1.3 %gather_fusion.1 = bf16[2,2,128,256]{3,2,1,0:T(8,128)(2,1)} fusion(bf16[4,2,128,256]{3,2,1,0:T(8,128)(2,1)S(1)} %get-tuple-element.10, s32[1024]{0:T(1024)S(1)} %pad_clamp_fusion), kind=kCustom, calls=%fused_computation.1 | custom fusion | bytes 524296 | tf_op jit(solution)/shard_map/gather | solution.py:96
  44.5 0.4 pad_add_fusion
  44.9 1.0 %copy.33 = bf16[2,2,128,256]{3,2,1,0:T(8,128)(2,1)S(1)} copy(bf16[2,2,128,256]{3,2,0,1:T(8,128)(2,1)} %bitcast.91) | data formatting | bytes 524288 | tf_op jit(solution)/shard_map/transpose | solution.py:104
  45.9 4.0 %fusion.4 = (f32[2,1024]{1,0:T(2,128)S(1)}, f32[2,768,1024]{2,1,0:T(8,128)}) fusion(pred[1024,768]{0,1:T(8,128)(4,1)S(1)} %pad_add_fusion, bf16[2,1024,128]{2,1,0:T(8,128)(2,1)S(1)} %bitcast.92, bf16[2,512,256]{2,1,0:T(8,128)(2,1)S(1)} %bitcast.98, bf16[2,256,256]{2,1,0:T(8,128)(2,1)S(1)} %bitcast.101), kind=kOutput, calls=%fused_computation.11 | convolution fusion | flops 408156160 | bytes 8396800 | tf_op jit(solution)/shard_map/gqd,gkd->gqk/dot_general | solution.py:30
  49.9 22.3 %all-gather.3.cloned.1.call-done = bf16[8,2,128,256]{3,2,1,0:T(8,128)(2,1)} async-done(((bf16[2,2,128,256]{3,2,1,0:T(8,128)(2,1)}), bf16[8,2,128,256]{3,2,1,0:T(8,128)(2,1)}) %all-gather.3.cloned.1.call-update) | async-done | bytes 1048592 | tf_op jit(solution)/shard_map/all_gather | solution.py:98
  72.2 1.3 %copy.36 = bf16[2,8,128,256]{3,2,1,0:T(8,128)(2,1)S(1)} copy(bf16[2,8,128,256]{3,2,0,1:T(8,128)(2,1)} %bitcast.96) | data formatting | bytes 2097152 | tf_op jit(solution)/shard_map/transpose | solution.py:130
  73.6 1.9 %bitcast_reduce_fusion = (f32[2,1024]{1,0:T(2,128)S(1)}, f32[2,1024,1024]{2,1,0:T(8,128)S(1)}) fusion(pred[1024]{0:T(1024)(128)(4,1)S(1)} %broadcast_bitcast_fusion.1, bf16[2,1024,128]{2,1,0:T(8,128)(2,1)S(1)} %bitcast.93, bf16[2,1024,256]{2,1,0:T(8,128)(2,1)S(1)} %bitcast.89), kind=kOutput, calls=%fused_computation.3 | convolution fusion | flops 543160320 | bytes 9446400 | tf_op jit(solution)/shard_map/gqd,gkd->gqk/dot_general | solution.py:30
  75.5 2.5 %fusion.2 = f32[2,1024]{1,0:T(2,128)S(1)} fusion(f32[2,1024,1024]{2,1,0:T(8,128)S(1)} %get-tuple-element.22, f32[2,1024]{1,0:T(2,128)S(1)} %get-tuple-element.17, pred[1024]{0:T(1024)(128)(4,1)S(1)} %broadcast_bitcast_fusion.1), kind=kLoop, calls=%fused_computation.9 | loop fusion | flops 10483712 | bytes 8406016 | tf_op jit(solution)/shard_map/reduce_sum | solution.py:36
  78.0 1.7 %fusion.5 = f32[2,1024]{1,0:T(2,128)S(1)} fusion(f32[2,768,1024]{2,1,0:T(8,128)S(1)} %bitcast.88, f32[2,1024]{1,0:T(2,128)S(1)} %get-tuple-element.18, pred[1024,768]{0,1:T(8,128)(4,1)S(1)} %pad_add_fusion), kind=kLoop, calls=%fused_computation.12 | loop fusion | flops 7862272 | bytes 7094272 | tf_op jit(solution)/shard_map/reduce_sum | solution.py:36
  79.7 2.8 %fusion.20 = f32[2,1024,128]{2,1,0:T(8,128)S(1)} fusion(f32[2,768,1024]{2,1,0:T(8,128)S(1)} %bitcast.88, f32[2,1024]{1,0:T(2,128)S(1)} %get-tuple-element.18, pred[1024,768]{0,1:T(8,128)(4,1)S(1)} %pad_add_fusion, f32[2,1024]{1,0:T(2,128)S(1)} %get-tuple-element.6, f32[2,1024]{1,0:T(2,128)S(1)} %get-tuple-element.16, ...), kind=kOutput, calls=%fused_computation.30 | convolution fusion | flops 411828224 | bytes 8937472 | tf_op jit(solution)/shard_map/gqk,gkd->gqd/dot_general | solution.py:37
  82.5 3.0 %divide_convert_fusion = bf16[2,1024,128]{2,1,0:T(8,128)(2,1)S(1)} fusion(f32[2,1024,128]{2,1,0:T(8,128)S(1)} %fusion.20, f32[2,1024,1024]{2,1,0:T(8,128)S(1)} %get-tuple-element.22, f32[2,1024]{1,0:T(2,128)S(1)} %get-tuple-element.17, pred[1024]{0:T(1024)(128)(4,1)S(1)} %broadcast_bitcast_fusion.1, bf16[2,1024,256]{2,1,0:T(8,128)(2,1)S(1)} %bitcast.90, ...), kind=kOutput, calls=%fused_computation.31 | convolution fusion | flops 548143104 | bytes 10504192 | tf_op jit(solution)/shard_map/gqk,gkd->gqd/dot_general | solution.py:37
  85.9 0.9 copy.44
  (47 shorter events, 2.6 us)
Async XLA Ops:
  6.5 65.7 %all-gather.3.cloned.1.call-start = ((), (), s32[]{:S(2)}) async-start(), calls=%async_computation | async-start | bytes 1310720 | tf_op jit(solution)/shard_map/all_gather | solution.py:98
  15.1 27.5 %collective-permute-start.2 = (bf16[1,2,256,256]{3,2,1,0:T(8,128)(2,1)S(1)}, bf16[1,2,256,256]{3,2,1,0:T(8,128)(2,1)S(1)}, u32[]{:S(2)}, u32[]{:S(2)}) collective-permute-start(bf16[1,2,256,256]{3,2,1,0:T(8,128)(2,1)S(1)} %get-tuple-element.12), channel_id=1, source_target_pairs={{0,12},{4,8},{8,4},{12,0},{1,13},{5,9},{9,5},{13,1},{2,14},{6,10},... | collective-permute-start | bytes 786440 | tf_op jit(solution)/shard_map/ppermute | solution.py:21
  20.3 13.1 %collective-permute-start = (bf16[1,2,256,256]{3,2,1,0:T(8,128)(2,1)S(1)}, bf16[1,2,256,256]{3,2,1,0:T(8,128)(2,1)S(1)}, u32[]{:S(2)}, u32[]{:S(2)}) collective-permute-start(bf16[1,2,256,256]{3,2,1,0:T(8,128)(2,1)S(1)} %get-tuple-element.14), channel_id=1, source_target_pairs={{0,4},{4,0},{8,12},{12,8},{1,5},{5,1},{9,13},{13,9},{2,6},{6,2},{1... | collective-permute-start | bytes 786440 | tf_op jit(solution)/shard_map/ppermute | solution.py:21
  20.3 22.3 %collective-permute-start.1 = (bf16[1,2,256,256]{3,2,1,0:T(8,128)(2,1)S(1)}, bf16[1,2,256,256]{3,2,1,0:T(8,128)(2,1)S(1)}, u32[]{:S(2)}, u32[]{:S(2)}) collective-permute-start(bf16[1,2,256,256]{3,2,1,0:T(8,128)(2,1)S(1)} %get-tuple-element.15), channel_id=1, source_target_pairs={{0,8},{4,12},{8,0},{12,4},{1,9},{5,13},{9,1},{13,5},{2,10},{6,14},... | collective-permute-start | bytes 786440 | tf_op jit(solution)/shard_map/ppermute | solution.py:21
  73.5 4.5 %slice-start = ((s8[6291456]{0:T(1024)(128)(4,1)}), s8[4194304]{0:T(1024)(128)(4,1)S(1)}, s32[]{:S(2)}) async-start(s8[6291456]{0:T(1024)(128)(4,1)} %bitcast.87), calls=%async_computation.1 | async-start | bytes 8388608
  73.5 4.5 %slice-start.1 = ((s8[6291456]{0:T(1024)(128)(4,1)}), s8[2097152]{0:T(1024)(128)(4,1)S(1)}, s32[]{:S(2)}) async-start(s8[6291456]{0:T(1024)(128)(4,1)} %bitcast.87), calls=%async_computation.2 | async-start | bytes 4194304
Sparse Core Ops, SparseCore 0:
  44.1 28.0 all-gather.2
